TPU v7x, 256 devices: a whole 4x4x8 slice. The times are simulated.
256 devices in a mesh: dp: 64 (over x, z, core), tensor: 4 (over y).
Axes of the slice: x: 4, y: 4, z: 8, core: 2. Of those that a mesh axis runs over, the one named last changes fastest.
Arguments:
- attention_grads: bfloat16 [64, 1, 512, 2048], P('dp', None, None, 'tensor')
- expert_grads: bfloat16 [64, 1, 2, 512, 4096], P('dp', None, None, None, 'tensor')
- routing_grads: bfloat16 [64, 4, 1, 36, 512], P('dp', 'tensor'), may hold values from -640 to 640
- attention_master: float32 [512, 2048], P('dp', 'tensor'), may hold values from -0.25 to 0.25
- attention_first: float32 [512, 2048], P('dp', 'tensor'), may hold values from -4 to 4
- attention_second: float32 [512, 2048], P('dp', 'tensor'), may hold values from 0.05 to 2
- expert_master: float32 [2, 512, 4096], P(None, 'dp', 'tensor'), may hold values from -0.25 to 0.25
- expert_first: float32 [2, 512, 4096], P(None, 'dp', 'tensor'), may hold values from -4 to 4
- expert_second: float32 [2, 512, 4096], P(None, 'dp', 'tensor'), may hold values from 0.05 to 2
- routing_master: float32 [36, 512], P(None, ('dp', 'tensor')), may hold values from -4 to 4
- routing_first: float32 [36, 512], P(None, ('dp', 'tensor')), may hold values from -4 to 4
- routing_second: float32 [36, 512], P(None, ('dp', 'tensor')), may hold values from 0.05 to 2
- step_count: int32 [1], replicated, may hold values from 1 to 1000
- learn_rate: float32 [1], replicated, may hold values from 0.05 to 0.3
- clip_level: float32 [1], replicated, may hold values from 0.5 to 2
Outputs:
- attention_renewed: float32 [512, 2048], P('dp', 'tensor')
- attention_momentum: float32 [512, 2048], P('dp', 'tensor')
- attention_variance: float32 [512, 2048], P('dp', 'tensor')
- attention_served: bfloat16 [512, 2048], P(None, 'tensor')
- expert_renewed: float32 [2, 512, 4096], P(None, 'dp', 'tensor')
- expert_momentum: float32 [2, 512, 4096], P(None, 'dp', 'tensor')
- expert_variance: float32 [2, 512, 4096], P(None, 'dp', 'tensor')
- expert_served: bfloat16 [2, 512, 4096], P(None, None, 'tensor')
- routing_renewed: float32 [36, 512], P(None, ('dp', 'tensor'))
- routing_momentum: float32 [36, 512], P(None, ('dp', 'tensor'))
- routing_variance: float32 [36, 512], P(None, ('dp', 'tensor'))
- routing_served: bfloat16 [36, 512], replicated
Inputs may be any that keep to these rules, and one draw needn't show every extreme that they name: `step_count`: the number of optimizer steps taken, this one included.
All inputs are finite; a program needn't handle non-finite values.
Results may differ from a plain program's by a relative error of at most 0.0004.
Values may be sent and summed in bfloat16 or wider, within the bound.
No kernel may reach another device: no remote copies, remote signals or barrier semaphores. Data moves between devices by JAX's collectives and lax.ppermute only.
A program may use at most 64 MiB of HBM per device.

v0:
```python
import jax
import jax.numpy as jnp
from jax import lax
from jax.sharding import Mesh, PartitionSpec as P

EXPERTS = 32
PARAMS = 5261312
BETA_ONE = 0.9
BETA_TWO = 0.999
EPSILON = 1e-08
DECAY = 0.1
DP_PARTS = ("dp_x", "dp_z", "dp_core")
DP = DP_PARTS


def adam_update(grad_sum, master, first, second, clip, rate, first_fix, second_fix, mask):
    grad = clip * grad_sum
    momentum = BETA_ONE * first + (1.0 - BETA_ONE) * grad
    variance = BETA_TWO * second + (1.0 - BETA_TWO) * grad * grad
    update = (
        momentum / first_fix / (jnp.sqrt(variance / second_fix) + EPSILON) + DECAY * mask * master
    )
    renewed = master - rate * update
    return (renewed, momentum, variance, renewed.astype(jnp.bfloat16))


def local(
    attention_grads,
    expert_grads,
    routing_grads,
    attention_master,
    attention_first,
    attention_second,
    expert_master,
    expert_first,
    expert_second,
    routing_master,
    routing_first,
    routing_second,
    step_count,
    learn_rate,
    clip_level,
):
    n_dp = lax.axis_size(DP)
    n_t = lax.axis_size("tensor")
    t_idx = lax.axis_index("tensor")
    att = attention_grads[0, 0]
    exp = expert_grads[0, 0]
    rte = routing_grads[0, 0, 0]
    rows, cols = att.shape
    n_e, e_rows, e_cols = exp.shape
    n_r, r_cols = rte.shape
    ra = rows // n_dp
    re = e_rows // n_dp
    rc = r_cols // n_dp
    own = rc // n_t
    exp_rows = exp.transpose(1, 0, 2).reshape(e_rows, n_e * e_cols)
    send = jnp.concatenate([att, exp_rows, rte.T], axis=1)
    got = lax.all_to_all(send, DP, 0, 0, tiled=True)
    total = jnp.sum(got.reshape(n_dp, ra, -1).astype(jnp.float32), axis=0)
    attention_sum = total[:, :cols]
    expert_sum = total[:, cols : cols + n_e * e_cols].reshape(re, n_e, e_cols).transpose(1, 0, 2)
    route_part = total[:, cols + n_e * e_cols :].T
    local_squares = jnp.sum(attention_sum * attention_sum) + jnp.sum(expert_sum * expert_sum)
    slot = (jnp.arange(rc) // own == t_idx)[None, :]

    def placed(values):
        return jnp.where(slot, jnp.tile(values, (1, n_t)), 0.0)

    packed = jnp.stack(
        [
            route_part,
            placed(routing_master),
            placed(routing_first),
            placed(routing_second),
            jnp.full((n_r, rc), 0.0).at[0, 0].set(local_squares),
        ]
    )
    packed = lax.psum(packed, "tensor")
    route_sum = packed[0]
    route_master_blk, route_first_blk, route_second_blk = (packed[1], packed[2], packed[3])
    group_squares = packed[4, 0, 0] + jnp.sum(route_sum * route_sum)
    spread = jnp.broadcast_to(group_squares, (n_dp, 1))
    squares = jnp.sum(lax.all_to_all(spread, DP, 0, 0, tiled=True))
    grad_norm = jnp.sqrt(squares)
    clip = jnp.minimum(1.0, clip_level[0] * jnp.sqrt(jnp.float32(PARAMS)) / (grad_norm + 1e-06))
    steps_done = step_count[0].astype(jnp.float32)
    first_fix = 1.0 - jnp.power(jnp.float32(BETA_ONE), steps_done)
    second_fix = 1.0 - jnp.power(jnp.float32(BETA_TWO), steps_done)
    rate = learn_rate[0]
    one = jnp.float32(1.0)
    attention_out = adam_update(
        attention_sum,
        attention_master,
        attention_first,
        attention_second,
        clip,
        rate,
        first_fix,
        second_fix,
        one,
    )
    expert_out = adam_update(
        expert_sum,
        expert_master,
        expert_first,
        expert_second,
        clip,
        rate,
        first_fix,
        second_fix,
        one,
    )
    row_index = jnp.arange(n_r, dtype=jnp.int32)
    routing_mask = (row_index < EXPERTS).astype(jnp.float32)[:, None]
    routing_out = adam_update(
        route_sum,
        route_master_blk,
        route_first_blk,
        route_second_blk,
        clip,
        rate,
        first_fix,
        second_fix,
        routing_mask,
    )

    def mine(values):
        return lax.dynamic_slice_in_dim(values, t_idx * own, own, axis=1)

    def gather(values):
        for name in (DP_PARTS[2], DP_PARTS[1]):
            values = lax.all_gather(values, name, axis=0, tiled=True)
        name = DP_PARTS[0]
        size = lax.axis_size(name)
        ring = [values] + [
            lax.ppermute(values, name, [(i, (i + size - k) % size) for i in range(size)])
            for k in range(1, size)
        ]
        stacked = jnp.stack(ring)
        stacked = jnp.roll(stacked, lax.axis_index(name), axis=0)
        return stacked.reshape((-1,) + values.shape[1:])

    rest = jnp.concatenate(
        [
            attention_out[3],
            expert_out[3].transpose(1, 0, 2).reshape(re, n_e * e_cols),
            routing_out[3].T,
        ],
        axis=1,
    )
    rest = gather(rest)
    attention_served = rest[:, :cols]
    expert_served = (
        rest[:, cols : cols + n_e * e_cols].reshape(e_rows, n_e, e_cols).transpose(1, 0, 2)
    )
    routing_served = rest[:, cols + n_e * e_cols :].T
    return (
        attention_out[0],
        attention_out[1],
        attention_out[2],
        attention_served,
        expert_out[0],
        expert_out[1],
        expert_out[2],
        expert_served,
        mine(routing_out[0]),
        mine(routing_out[1]),
        mine(routing_out[2]),
        routing_served,
    )


def split_mesh(mesh):
    column = mesh.devices[:, 0]
    sizes = (
        len({d.coords[0] for d in column}),
        len({d.coords[2] for d in column}),
        len({d.core_on_chip for d in column}),
    )
    devices = mesh.devices.reshape(sizes + mesh.devices.shape[1:])
    return Mesh(devices, DP_PARTS + ("tensor",))


def solution(mesh):
    mesh = split_mesh(mesh)
    in_specs = (
        P(DP, None, None, "tensor"),
        P(DP, None, None, None, "tensor"),
        P(DP, "tensor", None, None, None),
        P(DP, "tensor"),
        P(DP, "tensor"),
        P(DP, "tensor"),
        P(None, DP, "tensor"),
        P(None, DP, "tensor"),
        P(None, DP, "tensor"),
        P(None, DP + ("tensor",)),
        P(None, DP + ("tensor",)),
        P(None, DP + ("tensor",)),
        P(),
        P(),
        P(),
    )
    out_specs = (
        P(DP, "tensor"),
        P(DP, "tensor"),
        P(DP, "tensor"),
        P(None, "tensor"),
        P(None, DP, "tensor"),
        P(None, DP, "tensor"),
        P(None, DP, "tensor"),
        P(None, None, "tensor"),
        P(None, DP + ("tensor",)),
        P(None, DP + ("tensor",)),
        P(None, DP + ("tensor",)),
        P(),
    )
    return jax.shard_map(local, mesh=mesh, in_specs=in_specs, out_specs=out_specs, check_vma=False)
```

profile of v0, /device:TPU:7, one launch (start us, length us, event | category | flops | bytes accessed | tf_op | source)
XLA Modules:
  0.0 199.6 jit_solution(18282332297180285942)
XLA Ops:
  0.7 1.0 copy.75
  1.6 5.1 %copy.74 = bf16[512,2,1024]{2,1,0:T(2,128)(2,1)} copy(bf16[512,2,1024]{2,0,1:T(8,128)(2,1)} %bitcast.80) | data formatting | bytes 4194304 | tf_op jit(solution)/shard_map/transpose | solution.py:57
  6.7 3.3 %concatenate.21 = bf16[64,8,2048]{2,1,0:T(8,128)(2,1)S(1)} reshape(bf16[512,2,1024]{2,1,0:T(2,128)(2,1)} %copy.74) | data formatting | bytes 4194304 | tf_op jit(solution)/shard_map/concatenate | solution.py:58
  10.0 1.8 pad_maximum_fusion
  11.9 12.6 %all-to-all-start = ((bf16[64,8,2596]{2,1,0:T(8,128)(2,1)}), bf16[64,8,2596]{2,1,0:T(8,128)(2,1)S(1)}, u32[]{:S(2)}, u32[]{:S(2)}) async-start(bf16[64,8,2596]{2,1,0:T(8,128)(2,1)} %pad_maximum_fusion), calls=%async_computation | async-start | bytes 5505024 | tf_op jit(solution)/shard_map/all_to_all | solution.py:59
  26.4 62.9 %all-to-all-done = bf16[64,8,2596]{2,1,0:T(8,128)(2,1)S(1)} async-done(((bf16[64,8,2596]{2,1,0:T(8,128)(2,1)}), bf16[64,8,2596]{2,1,0:T(8,128)(2,1)S(1)}, u32[]{:S(2)}, u32[]{:S(2)}) %all-to-all-start) | async-done | bytes 2658336 | tf_op jit(solution)/shard_map/all_to_all | solution.py:59
  92.7 13.5 %psum.7 = f32[5,36,8]{1,2,0:T(8,128)S(1)} all-reduce(f32[5,36,8]{1,2,0:T(8,128)S(1)} %constant_dynamic-update-slice_fusion), channel_id=1, replica_groups=mesh['dp_x'=4,'dp_z'=8,'dp_core'=2,'tensor'=4] {'tensor'}, use_global_device_ids=true, to_apply=%region_3.4 | all-reduce | flops 1440 | bytes 11520 | tf_op jit(solution)/shard_map/psum | solution.py:79
  109.2 9.5 %all-to-all-start.1 = ((f32[64,1,1]{2,1,0:T(1,128)}), f32[64,1,1]{2,1,0:T(1,128)S(1)}, u32[]{:S(2)}, u32[]{:S(2)}) async-start(f32[64,1,1]{2,1,0:T(1,128)} %broadcast_in_dim.28), calls=%async_computation.1 | async-start | bytes 65536 | tf_op jit(solution)/shard_map/all_to_all | solution.py:84
  118.8 7.2 %all-to-all-done.1 = f32[64,1,1]{2,1,0:T(1,128)S(1)} async-done(((f32[64,1,1]{2,1,0:T(1,128)}), f32[64,1,1]{2,1,0:T(1,128)S(1)}, u32[]{:S(2)}, u32[]{:S(2)}) %all-to-all-start.1) | async-done | bytes 288 | tf_op jit(solution)/shard_map/all_to_all | solution.py:84
  128.8 2.2 %all_gather.6 = bf16[16,2596]{1,0:T(8,128)(2,1)S(1)} all-gather(bf16[8,2596]{1,0:T(8,128)(2,1)S(1)} %pad_maximum_fusion.1), channel_id=1, replica_groups=mesh['dp_x'=4,'dp_z'=8,'dp_core'=2,'tensor'=4] {'dp_core'}, dimensions={0}, use_global_device_ids=true | all-gather | bytes 124608 | tf_op jit(solution)/shard_map/all_gather | solution.py:133
  131.0 20.1 %all_gather.7 = bf16[128,2596]{1,0:T(8,128)(2,1)S(1)} all-gather(bf16[16,2596]{1,0:T(8,128)(2,1)S(1)} %all_gather.6), channel_id=1, replica_groups=mesh['dp_x'=4,'dp_z'=8,'dp_core'=2,'tensor'=4] {'dp_z'}, dimensions={0}, use_global_device_ids=true | all-gather | bytes 747648 | tf_op jit(solution)/shard_map/all_gather | solution.py:133
  151.4 2.0 collective-permute-start.2
  155.5 0.9 bitcast_dynamic-update-slice_fusion.4
  156.4 5.6 %collective-permute-done.2 = bf16[128,2596]{0,1:T(8,128)(2,1)S(1)} collective-permute-done((bf16[128,2596]{0,1:T(8,128)(2,1)S(1)}, bf16[128,2596]{0,1:T(8,128)(2,1)S(1)}, u32[]{:S(2)}, u32[]{:S(2)}) %collective-permute-start.2) | collective-permute-done | bytes 664608 | tf_op jit(solution)/shard_map/ppermute | solution.py:137
  162.4 23.8 %collective-permute-done = bf16[128,2596]{0,1:T(8,128)(2,1)} collective-permute-done((bf16[128,2596]{0,1:T(8,128)(2,1)S(1)}, bf16[128,2596]{0,1:T(8,128)(2,1)}, u32[]{:S(2)}, u32[]{:S(2)}) %collective-permute-start) | collective-permute-done | bytes 664608 | tf_op jit(solution)/shard_map/ppermute | solution.py:137
  186.1 1.4 copy.78
  187.6 0.9 bitcast_dynamic-update-slice_fusion.2
  188.8 0.9 bitcast_dynamic-update-slice_fusion
  189.7 0.9 constant_dynamic-update-slice_fusion.6
  190.6 0.9 bitcast_dynamic-update-slice_fusion.5
  191.5 0.9 bitcast_dynamic-update-slice_fusion.3
  192.5 0.9 bitcast_dynamic-update-slice_fusion.1
  194.3 2.0 constant_dynamic-slice_fusion.3
  198.1 1.5 copy.89
  (55 shorter events, 11.7 us)
Async XLA Ops:
  0.6 9.4 %copy-start = (bf16[1,1,512,512]{3,2,1,0:T(8,128)(2,1)S(1)}, bf16[1,1,512,512]{3,2,1,0:T(8,128)(2,1)}, u32[]{:S(2)}) copy-start(bf16[1,1,512,512]{3,2,1,0:T(8,128)(2,1)} %param.17) | copy-start | bytes 1572868
  11.8 80.7 %copy-start.7 = (f32[36,2]{0,1:T(2,128)S(1)}, f32[36,2]{0,1:T(2,128)}, u32[]{:S(2)}) copy-start(f32[36,2]{0,1:T(2,128)} %param.26) | copy-start | bytes 868
  11.8 80.7 %copy-start.8 = (f32[36,2]{0,1:T(2,128)S(1)}, f32[36,2]{0,1:T(2,128)}, u32[]{:S(2)}) copy-start(f32[36,2]{0,1:T(2,128)} %param.27) | copy-start | bytes 868
  11.8 80.8 %copy-start.9 = (f32[36,2]{0,1:T(2,128)S(1)}, f32[36,2]{0,1:T(2,128)}, u32[]{:S(2)}) copy-start(f32[36,2]{0,1:T(2,128)} %param.28) | copy-start | bytes 868
  11.8 115.6 %copy-start.4 = (f32[8,512]{1,0:T(8,128)S(1)}, f32[8,512]{1,0:T(8,128)}, u32[]{:S(2)}) copy-start(f32[8,512]{1,0:T(8,128)} %param.20) | copy-start | bytes 49156
  11.8 115.6 %copy-start.5 = (f32[8,512]{1,0:T(8,128)S(1)}, f32[8,512]{1,0:T(8,128)}, u32[]{:S(2)}) copy-start(f32[8,512]{1,0:T(8,128)} %param.22) | copy-start | bytes 49156
  11.8 115.6 %copy-start.6 = (f32[8,512]{1,0:T(8,128)S(1)}, f32[8,512]{1,0:T(8,128)}, u32[]{:S(2)}) copy-start(f32[8,512]{1,0:T(8,128)} %param.21) | copy-start | bytes 49156
  11.8 116.2 %copy-start.1 = (f32[2,8,1024]{2,1,0:T(8,128)S(1)}, f32[2,8,1024]{2,1,0:T(8,128)}, u32[]{:S(2)}) copy-start(f32[2,8,1024]{2,1,0:T(8,128)} %param.23) | copy-start | bytes 196612
  11.8 116.2 %copy-start.2 = (f32[2,8,1024]{2,1,0:T(8,128)S(1)}, f32[2,8,1024]{2,1,0:T(8,128)}, u32[]{:S(2)}) copy-start(f32[2,8,1024]{2,1,0:T(8,128)} %param.25) | copy-start | bytes 196612
  11.8 116.2 %copy-start.3 = (f32[2,8,1024]{2,1,0:T(8,128)S(1)}, f32[2,8,1024]{2,1,0:T(8,128)}, u32[]{:S(2)}) copy-start(f32[2,8,1024]{2,1,0:T(8,128)} %param.24) | copy-start | bytes 196612
  11.9 77.5 %all-to-all-start = ((bf16[64,8,2596]{2,1,0:T(8,128)(2,1)}), bf16[64,8,2596]{2,1,0:T(8,128)(2,1)S(1)}, u32[]{:S(2)}, u32[]{:S(2)}) async-start(bf16[64,8,2596]{2,1,0:T(8,128)(2,1)} %pad_maximum_fusion), calls=%async_computation | async-start | bytes 5505024 | tf_op jit(solution)/shard_map/all_to_all | solution.py:59
  109.2 16.7 %all-to-all-start.1 = ((f32[64,1,1]{2,1,0:T(1,128)}), f32[64,1,1]{2,1,0:T(1,128)S(1)}, u32[]{:S(2)}, u32[]{:S(2)}) async-start(f32[64,1,1]{2,1,0:T(1,128)} %broadcast_in_dim.28), calls=%async_computation.1 | async-start | bytes 65536 | tf_op jit(solution)/shard_map/all_to_all | solution.py:84
  151.4 10.6 %collective-permute-start.2 = (bf16[128,2596]{0,1:T(8,128)(2,1)S(1)}, bf16[128,2596]{0,1:T(8,128)(2,1)S(1)}, u32[]{:S(2)}, u32[]{:S(2)}) collective-permute-start(bf16[128,2596]{0,1:T(8,128)(2,1)S(1)} %copy.77), channel_id=1, source_target_pairs={{0,64},{64,128},{128,192},{192,0},{1,65},{65,129},{129,193},{193,1... | collective-permute-start | bytes 1993736 | tf_op jit(solution)/shard_map/ppermute | solution.py:137
  153.4 35.1 %collective-permute-start.1 = (bf16[128,2596]{0,1:T(8,128)(2,1)S(1)}, bf16[128,2596]{0,1:T(8,128)(2,1)S(1)}, u32[]{:S(2)}, u32[]{:S(2)}) collective-permute-start(bf16[128,2596]{0,1:T(8,128)(2,1)S(1)} %copy.77), channel_id=1, source_target_pairs={{0,128},{64,192},{128,0},{192,64},{1,129},{65,193},{129,1},{193,65... | collective-permute-start | bytes 1993736 | tf_op jit(solution)/shard_map/ppermute | solution.py:137
  154.0 32.2 %collective-permute-start = (bf16[128,2596]{0,1:T(8,128)(2,1)S(1)}, bf16[128,2596]{0,1:T(8,128)(2,1)}, u32[]{:S(2)}, u32[]{:S(2)}) collective-permute-start(bf16[128,2596]{0,1:T(8,128)(2,1)S(1)} %copy.77), channel_id=1, source_target_pairs={{0,192},{64,0},{128,64},{192,128},{1,193},{65,1},{129,65},{193,129... | collective-permute-start | bytes 1993736 | tf_op jit(solution)/shard_map/ppermute | solution.py:137
where the time goes:
time: 200 us
  waiting for transfers between devices  99.5 us (50%)
  blocking collectives  35.8 us (18%)
  local copies, waits for them, and re-layouts  26.7 us (13%)
  starting transfers between devices  25 us (12%)
  other arithmetic  6.4 us (3%)
  between operations  6.24 us (3%)
    all_to_all x1, waiting for transfers between devices, local(): got = lax.all_to_all(send, DP, 0, 0, tiled=True)  62.9 us
    ppermute x3, waiting for transfers between devices, gather(): lax.ppermute(values, name, [(i, (i + size - k) % size) for i in range(siz...  29.4 us
    all_gather x2, blocking collectives, gather(): values = lax.all_gather(values, name, axis=0, tiled=True)  22.3 us
    psum x1, blocking collectives, local(): packed = lax.psum(packed, 'tensor')  13.5 us
    all_to_all x1, starting transfers between devices, local(): got = lax.all_to_all(send, DP, 0, 0, tiled=True)  12.6 us
    all_to_all x1, starting transfers between devices, local(): squares = jnp.sum(lax.all_to_all(spread, DP, 0, 0, tiled=True))  9.48 us
    all_to_all x1, waiting for transfers between devices, local(): squares = jnp.sum(lax.all_to_all(spread, DP, 0, 0, tiled=True))  7.16 us
    unnamed x29, local copies, waits for them, and re-layouts  7.15 us
  transfers between devices with their start and end apart: 5, of which 4 were waited for; matrix products, arithmetic and copies ran while one was open for 2% of the time, Pallas kernels for 0%

commit v1 on v0

--- a/solution.py
+++ b/solution.py
@@ -1,3 +1,4 @@
+import functools
 import jax
 import jax.numpy as jnp
 from jax import lax
@@ -11,6 +12,13 @@
 DECAY = 0.1
 DP_PARTS = ("dp_x", "dp_z", "dp_core")
 DP = DP_PARTS
+
+
+def settle_columns(m, link_axis):
+    return jax.lax.all_gather(m, link_axis).sum(axis=0)
+
+
+serve_pages = functools.partial(settle_columns, link_axis="tensor")
 
 
 def adam_update(grad_sum, master, first, second, clip, rate, first_fix, second_fix, mask):
@@ -76,7 +84,7 @@
             jnp.full((n_r, rc), 0.0).at[0, 0].set(local_squares),
         ]
     )
-    packed = lax.psum(packed, "tensor")
+    packed = serve_pages(packed)
     route_sum = packed[0]
     route_master_blk, route_first_blk, route_second_blk = (packed[1], packed[2], packed[3])
     group_squares = packed[4, 0, 0] + jnp.sum(route_sum * route_sum)

time: 200 us -> 195 us (0.975)
  blocking collectives: 35.8 us -> 31.8 us
    psum x1 -> x0, blocking collectives: 13.5 us -> none  [local(): packed = lax.psum(packed, 'tensor')]
    all_gather x0 -> x1, blocking collectives: none -> 9.52 us  [settle_columns(): return jax.lax.all_gather(m, link_axis).sum(axis=0)]
where the time goes in v1:
time: 195 us
  waiting for transfers between devices  99.5 us (51%)
  blocking collectives  31.8 us (16%)
  local copies, waits for them, and re-layouts  26.7 us (14%)
  starting transfers between devices  24.2 us (12%)
  other arithmetic  6.42 us (3%)
  between operations  6.24 us (3%)
    all_to_all x1, waiting for transfers between devices, local(): got = lax.all_to_all(send, DP, 0, 0, tiled=True)  62.9 us
    ppermute x3, waiting for transfers between devices, gather(): lax.ppermute(values, name, [(i, (i + size - k) % size) for i in range(siz...  29.4 us
    all_gather x2, blocking collectives, gather(): values = lax.all_gather(values, name, axis=0, tiled=True)  22.3 us
    all_to_all x1, starting transfers between devices, local(): got = lax.all_to_all(send, DP, 0, 0, tiled=True)  12.6 us
    all_gather x1, blocking collectives, settle_columns(): return jax.lax.all_gather(m, link_axis).sum(axis=0)  9.52 us
    all_to_all x1, starting transfers between devices, local(): squares = jnp.sum(lax.all_to_all(spread, DP, 0, 0, tiled=True))  8.61 us
    all_to_all x1, waiting for transfers between devices, local(): squares = jnp.sum(lax.all_to_all(spread, DP, 0, 0, tiled=True))  7.16 us
    unnamed x29, local copies, waits for them, and re-layouts  7.15 us
  transfers between devices with their start and end apart: 5, of which 4 were waited for; matrix products, arithmetic and copies ran while one was open for 2% of the time, Pallas kernels for 0%

profile of v1, /device:TPU:7, one launch (start us, length us, event | category | flops | bytes accessed | tf_op | source)
XLA Modules:
  0.0 194.8 jit_solution(13754728327132670927)
XLA Ops:
  0.7 1.0 copy.75
  1.6 5.1 %copy.74 = bf16[512,2,1024]{2,1,0:T(2,128)(2,1)} copy(bf16[512,2,1024]{2,0,1:T(8,128)(2,1)} %bitcast.81) | data formatting | bytes 4194304 | tf_op jit(solution)/shard_map/transpose | solution.py:65
  6.7 3.3 %concatenate.21 = bf16[64,8,2048]{2,1,0:T(8,128)(2,1)S(1)} reshape(bf16[512,2,1024]{2,1,0:T(2,128)(2,1)} %copy.74) | data formatting | bytes 4194304 | tf_op jit(solution)/shard_map/concatenate | solution.py:66
  10.0 1.8 pad_maximum_fusion
  11.9 12.6 %all-to-all-start = ((bf16[64,8,2596]{2,1,0:T(8,128)(2,1)}), bf16[64,8,2596]{2,1,0:T(8,128)(2,1)S(1)}, u32[]{:S(2)}, u32[]{:S(2)}) async-start(bf16[64,8,2596]{2,1,0:T(8,128)(2,1)} %pad_maximum_fusion), calls=%async_computation | async-start | bytes 5505024 | tf_op jit(solution)/shard_map/all_to_all | solution.py:67
  26.4 62.9 %all-to-all-done = bf16[64,8,2596]{2,1,0:T(8,128)(2,1)S(1)} async-done(((bf16[64,8,2596]{2,1,0:T(8,128)(2,1)}), bf16[64,8,2596]{2,1,0:T(8,128)(2,1)S(1)}, u32[]{:S(2)}, u32[]{:S(2)}) %all-to-all-start) | async-done | bytes 2658336 | tf_op jit(solution)/shard_map/all_to_all | solution.py:67
  92.7 9.5 %all-gather = f32[20,36,8]{1,2,0:T(8,128)S(1)} all-gather(f32[5,36,8]{1,2,0:T(8,128)S(1)} %constant_dynamic-update-slice_fusion), channel_id=2, replica_groups=mesh['dp_x'=4,'dp_z'=8,'dp_core'=2,'tensor'=4] {'tensor'}, dimensions={0}, use_global_device_ids=true | all-gather | bytes 28800 | tf_op jit(solution)/shard_map/all_gather | solution.py:18
  105.3 8.6 %all-to-all-start.1 = ((f32[64,1,1]{2,1,0:T(1,128)}), f32[64,1,1]{2,1,0:T(1,128)S(1)}, u32[]{:S(2)}, u32[]{:S(2)}) async-start(f32[64,1,1]{2,1,0:T(1,128)} %broadcast_in_dim.28), calls=%async_computation.1 | async-start | bytes 65536 | tf_op jit(solution)/shard_map/all_to_all | solution.py:92
  114.0 7.2 %all-to-all-done.1 = f32[64,1,1]{2,1,0:T(1,128)S(1)} async-done(((f32[64,1,1]{2,1,0:T(1,128)}), f32[64,1,1]{2,1,0:T(1,128)S(1)}, u32[]{:S(2)}, u32[]{:S(2)}) %all-to-all-start.1) | async-done | bytes 288 | tf_op jit(solution)/shard_map/all_to_all | solution.py:92
  124.0 2.2 %all_gather.14 = bf16[16,2596]{1,0:T(8,128)(2,1)S(1)} all-gather(bf16[8,2596]{1,0:T(8,128)(2,1)S(1)} %pad_maximum_fusion.1), channel_id=1, replica_groups=mesh['dp_x'=4,'dp_z'=8,'dp_core'=2,'tensor'=4] {'dp_core'}, dimensions={0}, use_global_device_ids=true | all-gather | bytes 124608 | tf_op jit(solution)/shard_map/all_gather | solution.py:141
  126.1 20.1 %all_gather.15 = bf16[128,2596]{1,0:T(8,128)(2,1)S(1)} all-gather(bf16[16,2596]{1,0:T(8,128)(2,1)S(1)} %all_gather.14), channel_id=1, replica_groups=mesh['dp_x'=4,'dp_z'=8,'dp_core'=2,'tensor'=4] {'dp_z'}, dimensions={0}, use_global_device_ids=true | all-gather | bytes 747648 | tf_op jit(solution)/shard_map/all_gather | solution.py:141
  146.6 2.0 %collective-permute-start.2 = (bf16[128,2596]{0,1:T(8,128)(2,1)S(1)}, bf16[128,2596]{0,1:T(8,128)(2,1)S(1)}, u32[]{:S(2)}, u32[]{:S(2)}) collective-permute-start(bf16[128,2596]{0,1:T(8,128)(2,1)S(1)} %copy.77), channel_id=1, source_target_pairs={{0,64},{64,128},{128,192},{192,0},{1,65},{65,129},{129,193},{193,1... | collective-permute-start | bytes 1993736 | tf_op jit(solution)/shard_map/ppermute | solution.py:145
  150.7 0.9 bitcast_dynamic-update-slice_fusion.4
  151.6 5.6 %collective-permute-done.2 = bf16[128,2596]{0,1:T(8,128)(2,1)S(1)} collective-permute-done((bf16[128,2596]{0,1:T(8,128)(2,1)S(1)}, bf16[128,2596]{0,1:T(8,128)(2,1)S(1)}, u32[]{:S(2)}, u32[]{:S(2)}) %collective-permute-start.2) | collective-permute-done | bytes 664608 | tf_op jit(solution)/shard_map/ppermute | solution.py:145
  157.6 23.8 %collective-permute-done = bf16[128,2596]{0,1:T(8,128)(2,1)} collective-permute-done((bf16[128,2596]{0,1:T(8,128)(2,1)S(1)}, bf16[128,2596]{0,1:T(8,128)(2,1)}, u32[]{:S(2)}, u32[]{:S(2)}) %collective-permute-start) | collective-permute-done | bytes 664608 | tf_op jit(solution)/shard_map/ppermute | solution.py:145
  181.3 1.4 copy.78
  182.8 0.9 bitcast_dynamic-update-slice_fusion.2
  184.0 0.9 bitcast_dynamic-update-slice_fusion
  184.9 0.9 constant_dynamic-update-slice_fusion.6
  185.8 0.9 bitcast_dynamic-update-slice_fusion.5
  186.7 0.9 bitcast_dynamic-update-slice_fusion.3
  187.6 0.9 bitcast_dynamic-update-slice_fusion.1
  189.5 2.0 %constant_dynamic-slice_fusion.3 = bf16[4,128,2596]{2,1,0:T(8,128)(2,1)S(1)} fusion(bf16[8,128,2596]{2,1,0:T(8,128)(2,1)} %constant_dynamic-update-slice_fusion.5, s32[]{:T(128)S(6)} %select_n.63), kind=kLoop, calls=%fused_computation.49 | loop fusion | bytes 5316612 | tf_op jit(solution)/shard_map/jit(_roll_dynamic)/dynamic_slice | solution.py:149
  193.3 1.5 copy.89
  (56 shorter events, 11.7 us)
Async XLA Ops:
  0.6 9.4 %copy-start = (bf16[1,1,512,512]{3,2,1,0:T(8,128)(2,1)S(1)}, bf16[1,1,512,512]{3,2,1,0:T(8,128)(2,1)}, u32[]{:S(2)}) copy-start(bf16[1,1,512,512]{3,2,1,0:T(8,128)(2,1)} %param.17) | copy-start | bytes 1572868
  11.8 80.7 %copy-start.7 = (f32[36,2]{0,1:T(2,128)S(1)}, f32[36,2]{0,1:T(2,128)}, u32[]{:S(2)}) copy-start(f32[36,2]{0,1:T(2,128)} %param.26) | copy-start | bytes 868
  11.8 80.7 %copy-start.8 = (f32[36,2]{0,1:T(2,128)S(1)}, f32[36,2]{0,1:T(2,128)}, u32[]{:S(2)}) copy-start(f32[36,2]{0,1:T(2,128)} %param.27) | copy-start | bytes 868
  11.8 80.8 %copy-start.9 = (f32[36,2]{0,1:T(2,128)S(1)}, f32[36,2]{0,1:T(2,128)}, u32[]{:S(2)}) copy-start(f32[36,2]{0,1:T(2,128)} %param.28) | copy-start | bytes 868
  11.8 110.8 %copy-start.4 = (f32[8,512]{1,0:T(8,128)S(1)}, f32[8,512]{1,0:T(8,128)}, u32[]{:S(2)}) copy-start(f32[8,512]{1,0:T(8,128)} %param.20) | copy-start | bytes 49156
  11.8 110.8 %copy-start.5 = (f32[8,512]{1,0:T(8,128)S(1)}, f32[8,512]{1,0:T(8,128)}, u32[]{:S(2)}) copy-start(f32[8,512]{1,0:T(8,128)} %param.22) | copy-start | bytes 49156
  11.8 110.8 %copy-start.6 = (f32[8,512]{1,0:T(8,128)S(1)}, f32[8,512]{1,0:T(8,128)}, u32[]{:S(2)}) copy-start(f32[8,512]{1,0:T(8,128)} %param.21) | copy-start | bytes 49156
  11.8 111.4 %copy-start.1 = (f32[2,8,1024]{2,1,0:T(8,128)S(1)}, f32[2,8,1024]{2,1,0:T(8,128)}, u32[]{:S(2)}) copy-start(f32[2,8,1024]{2,1,0:T(8,128)} %param.23) | copy-start | bytes 196612
  11.8 111.4 %copy-start.2 = (f32[2,8,1024]{2,1,0:T(8,128)S(1)}, f32[2,8,1024]{2,1,0:T(8,128)}, u32[]{:S(2)}) copy-start(f32[2,8,1024]{2,1,0:T(8,128)} %param.25) | copy-start | bytes 196612
  11.8 111.4 %copy-start.3 = (f32[2,8,1024]{2,1,0:T(8,128)S(1)}, f32[2,8,1024]{2,1,0:T(8,128)}, u32[]{:S(2)}) copy-start(f32[2,8,1024]{2,1,0:T(8,128)} %param.24) | copy-start | bytes 196612
  11.9 77.5 %all-to-all-start = ((bf16[64,8,2596]{2,1,0:T(8,128)(2,1)}), bf16[64,8,2596]{2,1,0:T(8,128)(2,1)S(1)}, u32[]{:S(2)}, u32[]{:S(2)}) async-start(bf16[64,8,2596]{2,1,0:T(8,128)(2,1)} %pad_maximum_fusion), calls=%async_computation | async-start | bytes 5505024 | tf_op jit(solution)/shard_map/all_to_all | solution.py:67
  105.3 15.9 %all-to-all-start.1 = ((f32[64,1,1]{2,1,0:T(1,128)}), f32[64,1,1]{2,1,0:T(1,128)S(1)}, u32[]{:S(2)}, u32[]{:S(2)}) async-start(f32[64,1,1]{2,1,0:T(1,128)} %broadcast_in_dim.28), calls=%async_computation.1 | async-start | bytes 65536 | tf_op jit(solution)/shard_map/all_to_all | solution.py:92
  146.6 10.6 %collective-permute-start.2 = (bf16[128,2596]{0,1:T(8,128)(2,1)S(1)}, bf16[128,2596]{0,1:T(8,128)(2,1)S(1)}, u32[]{:S(2)}, u32[]{:S(2)}) collective-permute-start(bf16[128,2596]{0,1:T(8,128)(2,1)S(1)} %copy.77), channel_id=1, source_target_pairs={{0,64},{64,128},{128,192},{192,0},{1,65},{65,129},{129,193},{193,1... | collective-permute-start | bytes 1993736 | tf_op jit(solution)/shard_map/ppermute | solution.py:145
  148.6 35.1 %collective-permute-start.1 = (bf16[128,2596]{0,1:T(8,128)(2,1)S(1)}, bf16[128,2596]{0,1:T(8,128)(2,1)S(1)}, u32[]{:S(2)}, u32[]{:S(2)}) collective-permute-start(bf16[128,2596]{0,1:T(8,128)(2,1)S(1)} %copy.77), channel_id=1, source_target_pairs={{0,128},{64,192},{128,0},{192,64},{1,129},{65,193},{129,1},{193,65... | collective-permute-start | bytes 1993736 | tf_op jit(solution)/shard_map/ppermute | solution.py:145
  149.2 32.2 %collective-permute-start = (bf16[128,2596]{0,1:T(8,128)(2,1)S(1)}, bf16[128,2596]{0,1:T(8,128)(2,1)}, u32[]{:S(2)}, u32[]{:S(2)}) collective-permute-start(bf16[128,2596]{0,1:T(8,128)(2,1)S(1)} %copy.77), channel_id=1, source_target_pairs={{0,192},{64,0},{128,64},{192,128},{1,193},{65,1},{129,65},{193,129... | collective-permute-start | bytes 1993736 | tf_op jit(solution)/shard_map/ppermute | solution.py:145
